TPU v7x, 512 devices: a whole 4x8x8 slice. The times are simulated.
512 devices in a mesh: dp: 16 (over z, core), expert: 32 (over x, y).
Axes of the slice: x: 4, y: 8, z: 8, core: 2. Of those that a mesh axis runs over, the one named last changes fastest.
Arguments:
- residual_in: bfloat16 [16384, 2048], P(('dp', 'expert')), may hold values from -6 to 6
- attention_out: bfloat16 [16384, 2048], P(('dp', 'expert')), may hold values from -6 to 6
- out_weight: bfloat16 [2048, 2048], P(None, 'dp'), may hold values from -0.125 to 0.125
- post_gain: float32 [2048], replicated, may hold values from 0.1 to 1.9
- router_weight: bfloat16 [2048, 32], replicated, may hold values from -0.125 to 0.125
- expert_ids: int32 [16384, 6], P(('dp', 'expert')), may hold values from 0 to 31, all different within a row; in each aligned block of 32 rows (0 to 31, 32 to 63, ...) at most 12 rows name the same one
- expert_slot: int32 [32], replicated, may hold values from 0 to 31, each once
- expert_gate_up: bfloat16 [32, 2048, 1408], P('expert', 'dp'), may hold values from -0.125 to 0.125
- expert_down: bfloat16 [32, 704, 2048], P('expert', None, 'dp'), may hold values from -0.21875 to 0.21875
- shared_gate_up: bfloat16 [2048, 2, 2816], P(None, None, 'dp'), may hold values from -0.125 to 0.125
- shared_down: bfloat16 [2816, 2048], P(None, 'dp'), may hold values from -0.109375 to 0.109375
- final_gain: float32 [2048], replicated, may hold values from 0.1 to 1.9
Outputs:
- mixed: bfloat16 [16384, 2048], P(('dp', 'expert'))
Inputs may be any that keep to these rules, and one draw needn't show every extreme that they name: `expert_ids`: each row names 6 different experts. In each aligned block of 32 rows (the rows of one device) no expert is named by more than 12 rows, a bound that some block reaches. A permutation: expert e is held in slot expert_slot[e].
All inputs are finite; a program needn't handle non-finite values.
Results may differ from a plain program's by a relative error of at most 0.0069.
Values may be sent and summed in bfloat16 or wider, within the bound.
No kernel may reach another device: no remote copies, remote signals or barrier semaphores. Data moves between devices by JAX's collectives and lax.ppermute only.
A program may use at most 64 MiB of HBM per device.

v0:
```python
import jax
import jax.numpy as jnp
from jax import lax
from jax.sharding import PartitionSpec as P

EPS = 1e-06


def core_groups(axis):
    n = lax.axis_size(axis)
    return [list(range(0, n, 2)), list(range(1, n, 2))]


def with_sibling(blocks, axis):
    other = lax.ppermute(blocks, axis, [(i, i ^ 1) for i in range(lax.axis_size(axis))])
    pair = jnp.stack([blocks, other], axis=1)
    pair = jnp.where(lax.axis_index(axis) % 2 == 0, pair, jnp.flip(pair, axis=1))
    return pair.reshape(-1, *blocks.shape[1:])


def pair_gather(array, axis):
    blocks = lax.all_gather(array, axis, axis=0, axis_index_groups=core_groups(axis))
    return with_sibling(blocks, axis)


def pair_collect(array, axis):
    copies = jnp.broadcast_to(array, (lax.axis_size(axis) // 2, *array.shape))
    blocks = lax.all_to_all(copies, axis, 0, 0, tiled=True, axis_index_groups=core_groups(axis))
    return with_sibling(blocks, axis)


def in_order(blocks, dim):
    shape = list(blocks.shape[1:])
    shape[dim] *= blocks.shape[0]
    return jnp.moveaxis(blocks, 0, dim).reshape(shape)


def sent_to_all(array, axis):
    copies = jnp.broadcast_to(array, (lax.axis_size(axis), *array.shape))
    return lax.all_to_all(copies, axis, split_axis=0, concat_axis=0, tiled=True)


def collect(array, axis, dim):
    return in_order(sent_to_all(array, axis), dim)


def turned_gather(arrays, axis, dims):
    turned = [jnp.moveaxis(a, dim, 0) for a, dim in zip(arrays, dims)]
    widths = [t[0].size for t in turned]
    both = jnp.concatenate([t.reshape(-1, w) for t, w in zip(turned, widths)], axis=1)
    out = lax.all_gather(both, axis, axis=0, tiled=True)
    blocks = jnp.split(out, [sum(widths[:k]) for k in range(1, len(widths))], axis=1)
    return tuple(
        (
            jnp.moveaxis(b.reshape(-1, *t.shape[1:]), 0, dim)
            for b, t, dim in zip(blocks, turned, dims)
        )
    )


def rms_scale(values, gain):
    values = values.astype(jnp.float32)
    inverse = lax.rsqrt(jnp.mean(values * values, axis=-1, keepdims=True) + EPS)
    return values * inverse * gain


def per_device(
    residual_in,
    attention_out,
    out_weight,
    post_gain,
    router_weight,
    expert_ids,
    expert_slot,
    expert_gate_up,
    expert_down,
    shared_gate_up,
    shared_down,
    final_gain,
):
    rows = residual_in.shape[0]
    width = residual_in.shape[1]
    experts = router_weight.shape[1]
    choose = expert_ids.shape[1]
    capacity = max(2, min(rows, 2 * rows * choose // experts))
    proj_cols = jnp.dot(
        in_order(pair_collect(attention_out, "dp"), 0),
        out_weight,
        preferred_element_type=jnp.float32,
    ).astype(jnp.bfloat16)
    proj = lax.all_to_all(proj_cols, "dp", split_axis=0, concat_axis=1, tiled=True)
    resid = (residual_in.astype(jnp.float32) + proj.astype(jnp.float32)).astype(jnp.bfloat16)
    normed = rms_scale(resid, post_gain).astype(jnp.bfloat16)
    logits = jnp.dot(normed, router_weight, preferred_element_type=jnp.float32)
    expert_range = jnp.arange(experts, dtype=jnp.int32)
    ids = expert_ids + (proj_cols[0, 0] * 0).astype(expert_ids.dtype)
    picked = ids[:, :, None] == expert_range[None, None, :]
    chosen = jnp.sum(jnp.where(picked, logits[:, None, :], 0.0), axis=2)
    raised = jnp.exp(chosen)
    gates = raised / jnp.sum(raised, axis=1, keepdims=True)
    slots = jnp.sum(jnp.where(picked, expert_slot[None, None, :], 0), axis=2).reshape(-1)
    marked = (slots[:, None] == expert_range[None, :]).astype(jnp.int32)
    before = jnp.cumsum(marked, axis=0) - marked
    position = jnp.sum(before * marked, axis=1)
    target = slots * capacity + position
    placed = target[:, None] == jnp.arange(experts * capacity, dtype=jnp.int32)[None, :]
    select = jnp.any(placed.reshape(rows, choose, experts * capacity), axis=1).astype(jnp.bfloat16)
    outgoing = jnp.einsum("rs,rd->sd", select, normed, preferred_element_type=jnp.float32)
    outgoing = outgoing.astype(jnp.bfloat16).reshape(experts, capacity, width)
    hidden_units = expert_down.shape[1]
    weights_part = jnp.concatenate([expert_gate_up[0], expert_down[0].T], axis=1)
    weights_full = lax.all_gather(weights_part, "dp", axis=0, tiled=True)
    gate_up_full = weights_full[:, : 2 * hidden_units]
    down_turned_full = weights_full[:, 2 * hidden_units :]
    received = lax.all_to_all(outgoing, "expert", split_axis=0, concat_axis=0, tiled=True)
    sources, count, _ = received.shape
    flat = received.reshape(sources * count, width)
    both = jnp.dot(flat, gate_up_full, preferred_element_type=jnp.float32)
    active = (jax.nn.silu(both[:, :hidden_units]) * both[:, hidden_units:]).astype(jnp.bfloat16)
    result = lax.dot_general(
        active, down_turned_full, (((1,), (1,)), ((), ())), preferred_element_type=jnp.float32
    ).astype(jnp.bfloat16)
    result = result.reshape(sources, count, width)
    returned = lax.all_to_all(result, "expert", split_axis=0, concat_axis=0, tiled=True)
    shared_units = shared_gate_up.shape[2]
    shared_pair = shared_gate_up.reshape(width, 2 * shared_units)
    normed_shared = normed + (weights_full[0, 0] * 0 + outgoing[0, 0, 0] * 0).astype(normed.dtype)
    both = jnp.dot(
        in_order(pair_gather(normed_shared, "dp"), 0),
        shared_pair,
        preferred_element_type=jnp.float32,
    )
    shared_hidden = (jax.nn.silu(both[:, :shared_units]) * both[:, shared_units:]).astype(
        jnp.bfloat16
    )
    out_cols = jnp.dot(
        in_order(pair_gather(shared_hidden, "dp"), 1),
        shared_down,
        preferred_element_type=jnp.float32,
    )
    shared_out = lax.all_to_all(
        out_cols.astype(jnp.bfloat16), "dp", split_axis=0, concat_axis=1, tiled=True
    ).astype(jnp.float32)
    weighted = jnp.sum(placed.reshape(rows, choose, experts * capacity) * gates[:, :, None], axis=1)
    routed = jnp.dot(
        weighted,
        returned.reshape(experts * capacity, width).astype(jnp.float32),
        precision=lax.Precision.HIGHEST,
        preferred_element_type=jnp.float32,
    )
    total = resid.astype(jnp.float32) + routed + shared_out
    return rms_scale(total, final_gain).astype(jnp.bfloat16)


def solution(mesh):
    in_specs = (
        P(("dp", "expert"), None),
        P(("dp", "expert"), None),
        P(None, "dp"),
        P(),
        P(),
        P(("dp", "expert"), None),
        P(),
        P("expert", "dp", None),
        P("expert", None, "dp"),
        P(None, None, "dp"),
        P(None, "dp"),
        P(),
    )
    out_specs = P(("dp", "expert"), None)
    return jax.shard_map(
        per_device, mesh=mesh, in_specs=in_specs, out_specs=out_specs, check_vma=False
    )
```

profile of v0, /device:TPU:1, one launch (start us, length us, event | category | flops | bytes accessed | tf_op | source)
XLA Modules:
  0.0 248.7 jit_solution(5507769714941726172)
XLA Ops:
  7.7 1.8 pad_maximum_fusion.3
  9.7 44.2 %all_to_all.41 = bf16[8,32,2048]{2,1,0:T(8,128)(2,1)S(1)} all-to-all(bf16[8,32,2048]{2,1,0:T(8,128)(2,1)S(1)} %broadcast_in_dim.26), channel_id=1, replica_groups={{0,64,128,192,256,320,384,448},{32,96,160,224,288,352,416,480},{1,65,12..., dimensions={0} | all-to-all | bytes 2097152 | tf_op jit(solution)/shard_map/all_to_all | solution.py:28
  53.9 5.5 %collective-permute-start = (bf16[8,32,2048]{2,1,0:T(8,128)(2,1)S(1)}, bf16[8,32,2048]{2,1,0:T(8,128)(2,1)S(1)}, u32[]{:S(2)}, u32[]{:S(2)}) collective-permute-start(bf16[8,32,2048]{2,1,0:T(8,128)(2,1)S(1)} %all_to_all.41), channel_id=1, source_target_pairs={{0,32},{32,0},{64,96},{96,64},{128,160},{160,128},{192,224},{224,1... | collective-permute-start | bytes 3145736 | tf_op jit(solution)/shard_map/ppermute | solution.py:15
  59.5 2.3 collective-permute-done
  66.1 3.7 %all-to-all-start.1 = ((bf16[16,32,128]{2,1,0:T(8,128)(2,1)}), bf16[16,32,128]{2,1,0:T(8,128)(2,1)S(1)}, u32[]{:S(2)}, u32[]{:S(2)}) async-start(bf16[16,32,128]{2,1,0:T(8,128)(2,1)} %bitcast.4), calls=%async_computation.1 | async-start | bytes 262144 | tf_op jit(solution)/shard_map/all_to_all | solution.py:91
  71.6 8.8 %all-to-all-done.1 = bf16[16,32,128]{2,1,0:T(8,128)(2,1)S(1)} async-done(((bf16[16,32,128]{2,1,0:T(8,128)(2,1)}), bf16[16,32,128]{2,1,0:T(8,128)(2,1)S(1)}, u32[]{:S(2)}, u32[]{:S(2)}) %all-to-all-start.1) | async-done | bytes 131104 | tf_op jit(solution)/shard_map/all_to_all | solution.py:91
  81.3 1.6 reshape.112
  84.7 8.7 %all-gather.6.cloned.1.call-done = bf16[2048,2112]{1,0:T(8,128)(2,1)} async-done(((bf16[128,2112]{1,0:T(8,128)(2,1)}), bf16[2048,2112]{1,0:T(8,128)(2,1)}) %all-gather.6.cloned.1.call-update) | async-done | bytes 8650768 | tf_op jit(solution)/shard_map/all_gather | solution.py:112
  96.1 9.7 %all-to-all-start.2 = ((bf16[32,12,2048]{2,1,0:T(8,128)(2,1)}), bf16[32,12,2048]{2,1,0:T(8,128)(2,1)S(1)}, u32[]{:S(2)}, u32[]{:S(2)}) async-start(bf16[32,12,2048]{2,1,0:T(8,128)(2,1)} %reshape.112), calls=%async_computation.2 | async-start | bytes 4194304 | tf_op jit(solution)/shard_map/all_to_all | solution.py:115
  105.8 26.9 %all-gather.8.cloned.1.call-done = bf16[256,2048]{1,0:T(8,128)(2,1)} async-done(((bf16[32,2048]{1,0:T(8,128)(2,1)}), bf16[256,2048]{1,0:T(8,128)(2,1)}) %all-gather.8.cloned.1.call-update) | async-done | bytes 1048592 | tf_op jit(solution)/shard_map/all_gather | solution.py:22
  132.8 6.4 %collective-permute-start.1 = (bf16[8,32,2048]{2,1,0:T(8,128)(2,1)}, bf16[8,32,2048]{2,1,0:T(8,128)(2,1)S(1)}, u32[]{:S(2)}, u32[]{:S(2)}) collective-permute-start(bf16[8,32,2048]{2,1,0:T(8,128)(2,1)} %bitcast.86), channel_id=1, source_target_pairs={{0,32},{32,0},{64,96},{96,64},{128,160},{160,128},{192,224},{224,1... | collective-permute-start | bytes 3145736 | tf_op jit(solution)/shard_map/ppermute | solution.py:15
  139.2 2.5 collective-permute-done.1
  145.4 9.3 %all-to-all-done.2 = bf16[32,12,2048]{2,1,0:T(8,128)(2,1)S(1)} async-done(((bf16[32,12,2048]{2,1,0:T(8,128)(2,1)}), bf16[32,12,2048]{2,1,0:T(8,128)(2,1)S(1)}, u32[]{:S(2)}, u32[]{:S(2)}) %all-to-all-start.2) | async-done | bytes 1572896 | tf_op jit(solution)/shard_map/all_to_all | solution.py:115
  156.0 5.8 %fusion = f32[384,1408]{1,0:T(8,128)S(1)} fusion(bf16[384,2048]{1,0:T(8,128)(2,1)} %reshape.113, bf16[2048,2112]{1,0:T(8,128)(2,1)} %all-gather.6.cloned.1.call-done), kind=kOutput, calls=%fused_computation | convolution fusion | flops 2214592512 | bytes 9502720 | tf_op jit(solution)/shard_map/dot_general | solution.py:118
  161.8 3.3 %fusion.4 = bf16[384,2048]{1,0:T(8,128)(2,1)S(1)} fusion(bf16[2048,2112]{1,0:T(8,128)(2,1)} %all-gather.6.cloned.1.call-done, f32[384,1408]{1,0:T(8,128)S(1)} %fusion), kind=kOutput, calls=%fused_computation.8 | convolution fusion | flops 1109704704 | bytes 7077888 | tf_op jit(solution)/shard_map/dot_general | solution.py:120
  166.7 7.5 %all-to-all-start.3 = ((bf16[32,12,2048]{2,1,0:T(8,128)(2,1)}), bf16[32,12,2048]{2,1,0:T(8,128)(2,1)S(1)}, u32[]{:S(2)}, u32[]{:S(2)}) async-start(bf16[32,12,2048]{2,1,0:T(8,128)(2,1)} %reshape.114), calls=%async_computation.3 | async-start | bytes 4194304 | tf_op jit(solution)/shard_map/all_to_all | solution.py:124
  174.2 7.8 %all-gather.10.cloned.1.call-done = bf16[4096,176]{0,1:T(8,128)(2,1)} async-done(((bf16[512,176]{0,1:T(8,128)(2,1)}), bf16[4096,176]{0,1:T(8,128)(2,1)}) %all-gather.10.cloned.1.call-update) | async-done | bytes 1441808 | tf_op jit(solution)/shard_map/all_gather | solution.py:22
  182.0 1.6 copy.60
  183.6 7.3 %collective-permute-start.2 = (bf16[8,512,176]{1,2,0:T(8,128)(2,1)S(1)}, bf16[8,512,176]{1,2,0:T(8,128)(2,1)S(1)}, u32[]{:S(2)}, u32[]{:S(2)}) collective-permute-start(bf16[8,512,176]{1,2,0:T(8,128)(2,1)S(1)} %bitcast.83), channel_id=1, source_target_pairs={{0,32},{32,0},{64,96},{96,64},{128,160},{160,128},{192,224},{224,1... | collective-permute-start | bytes 4325384 | tf_op jit(solution)/shard_map/ppermute | solution.py:15
  195.0 1.6 convolution_convert_fusion.2
  196.6 26.5 %all-to-all-done.3 = bf16[32,12,2048]{2,1,0:T(8,128)(2,1)S(1)} async-done(((bf16[32,12,2048]{2,1,0:T(8,128)(2,1)}), bf16[32,12,2048]{2,1,0:T(8,128)(2,1)S(1)}, u32[]{:S(2)}, u32[]{:S(2)}) %all-to-all-start.3) | async-done | bytes 1572896 | tf_op jit(solution)/shard_map/all_to_all | solution.py:124
  223.1 6.7 %all-to-all-start.4 = ((bf16[16,32,128]{2,1,0:T(8,128)(2,1)}), bf16[16,32,128]{2,1,0:T(8,128)(2,1)}, u32[]{:S(2)}, u32[]{:S(2)}) async-start(bf16[16,32,128]{2,1,0:T(8,128)(2,1)} %bitcast.90), calls=%async_computation.4 | async-start | bytes 262144 | tf_op jit(solution)/shard_map/all_to_all | solution.py:141
  231.8 7.2 %all-to-all-done.4 = bf16[16,32,128]{2,1,0:T(8,128)(2,1)} async-done(((bf16[16,32,128]{2,1,0:T(8,128)(2,1)}), bf16[16,32,128]{2,1,0:T(8,128)(2,1)}, u32[]{:S(2)}, u32[]{:S(2)}) %all-to-all-start.4) | async-done | bytes 131104 | tf_op jit(solution)/shard_map/all_to_all | solution.py:141
  239.0 2.4 multiply_reduce_fusion
  (83 shorter events, 24.2 us)
Async XLA Ops:
  6.5 137.1 %copy-start = (bf16[2048,2,176]{0,2,1:T(8,128)(2,1)S(1)}, bf16[2048,2,176]{0,2,1:T(8,128)(2,1)}, u32[]{:S(2)}) copy-start(bf16[2048,2,176]{0,2,1:T(8,128)(2,1)} %param.21) | copy-start | bytes 4325380
  6.5 3.0 %copy-start.6 = (bf16[32,2048]{1,0:T(8,128)(2,1)S(1)}, bf16[32,2048]{1,0:T(8,128)(2,1)}, u32[]{:S(2)}) copy-start(bf16[32,2048]{1,0:T(8,128)(2,1)} %param.13) | copy-start | bytes 393220
  6.5 86.9 %all-gather.6.cloned.1.call-start = ((), (), s32[]{:S(2)}) async-start(), calls=%async_computation.5 | async-start | bytes 9469952 | tf_op jit(solution)/shard_map/all_gather | solution.py:112
  53.9 7.8 %collective-permute-start = (bf16[8,32,2048]{2,1,0:T(8,128)(2,1)S(1)}, bf16[8,32,2048]{2,1,0:T(8,128)(2,1)S(1)}, u32[]{:S(2)}, u32[]{:S(2)}) collective-permute-start(bf16[8,32,2048]{2,1,0:T(8,128)(2,1)S(1)} %all_to_all.41), channel_id=1, source_target_pairs={{0,32},{32,0},{64,96},{96,64},{128,160},{160,128},{192,224},{224,1... | collective-permute-start | bytes 3145736 | tf_op jit(solution)/shard_map/ppermute | solution.py:15
  62.5 7.3 %copy-start.10 = (s32[32,6]{0,1:T(8,128)S(1)}, s32[32,6]{0,1:T(8,128)}, u32[]{:S(2)}) copy-start(s32[32,6]{0,1:T(8,128)} %param.17) | copy-start | bytes 2308
  62.6 7.3 %copy-start.13 = (s32[32]{0:T(128)S(1)}, s32[32]{0:T(128)}, u32[]{:S(2)}) copy-start(s32[32]{0:T(128)} %param.18) | copy-start | bytes 388
  62.6 17.9 %copy-start.7 = (bf16[32,2048]{1,0:T(8,128)(2,1)S(1)}, bf16[32,2048]{1,0:T(8,128)(2,1)}, u32[]{:S(2)}) copy-start(bf16[32,2048]{1,0:T(8,128)(2,1)} %param.12) | copy-start | bytes 393220
  62.6 18.1 %copy-start.8 = (f32[2048]{0:T(1024)S(1)}, f32[2048]{0:T(1024)}, u32[]{:S(2)}) copy-start(f32[2048]{0:T(1024)} %param.15) | copy-start | bytes 24580
  66.1 14.4 %all-to-all-start.1 = ((bf16[16,32,128]{2,1,0:T(8,128)(2,1)}), bf16[16,32,128]{2,1,0:T(8,128)(2,1)S(1)}, u32[]{:S(2)}, u32[]{:S(2)}) async-start(bf16[16,32,128]{2,1,0:T(8,128)(2,1)} %bitcast.4), calls=%async_computation.1 | async-start | bytes 262144 | tf_op jit(solution)/shard_map/all_to_all | solution.py:91
  69.8 63.0 %all-gather.8.cloned.1.call-start = ((), (), s32[]{:S(2)}) async-start(), calls=%async_computation.6 | async-start | bytes 1179648 | tf_op jit(solution)/shard_map/all_gather | solution.py:22
  80.6 14.7 %copy-start.2 = (bf16[32,2048]{1,0:T(8,128)(2,1)}, bf16[32,2048]{1,0:T(8,128)(2,1)S(1)}, u32[]{:S(2)}) copy-start(bf16[32,2048]{1,0:T(8,128)(2,1)S(1)} %get-tuple-element.6) | copy-start | bytes 393220
  80.6 14.6 %copy-start.11 = (f32[32]{0:T(128)}, f32[32]{0:T(128)S(1)}, u32[]{:S(2)}) copy-start(f32[32]{0:T(128)S(1)} %add_rsqrt_fusion.1) | copy-start | bytes 388
  96.1 58.6 %all-to-all-start.2 = ((bf16[32,12,2048]{2,1,0:T(8,128)(2,1)}), bf16[32,12,2048]{2,1,0:T(8,128)(2,1)S(1)}, u32[]{:S(2)}, u32[]{:S(2)}) async-start(bf16[32,12,2048]{2,1,0:T(8,128)(2,1)} %reshape.112), calls=%async_computation.2 | async-start | bytes 4194304 | tf_op jit(solution)/shard_map/all_to_all | solution.py:115
  105.8 76.3 %all-gather.10.cloned.1.call-start = ((), (), s32[]{:S(2)}) async-start(), calls=%async_computation.7 | async-start | bytes 1622016 | tf_op jit(solution)/shard_map/all_gather | solution.py:22
  132.8 8.9 %collective-permute-start.1 = (bf16[8,32,2048]{2,1,0:T(8,128)(2,1)}, bf16[8,32,2048]{2,1,0:T(8,128)(2,1)S(1)}, u32[]{:S(2)}, u32[]{:S(2)}) collective-permute-start(bf16[8,32,2048]{2,1,0:T(8,128)(2,1)} %bitcast.86), channel_id=1, source_target_pairs={{0,32},{32,0},{64,96},{96,64},{128,160},{160,128},{192,224},{224,1... | collective-permute-start | bytes 3145736 | tf_op jit(solution)/shard_map/ppermute | solution.py:15
  166.7 56.4 %all-to-all-start.3 = ((bf16[32,12,2048]{2,1,0:T(8,128)(2,1)}), bf16[32,12,2048]{2,1,0:T(8,128)(2,1)S(1)}, u32[]{:S(2)}, u32[]{:S(2)}) async-start(bf16[32,12,2048]{2,1,0:T(8,128)(2,1)} %reshape.114), calls=%async_computation.3 | async-start | bytes 4194304 | tf_op jit(solution)/shard_map/all_to_all | solution.py:124
  182.0 8.9 %copy-start.3 = (bf16[32,2048]{1,0:T(8,128)(2,1)S(1)}, bf16[32,2048]{1,0:T(8,128)(2,1)}, u32[]{:S(2)}) copy-start(bf16[32,2048]{1,0:T(8,128)(2,1)} %copy-done.2) | copy-start | bytes 393220
  182.0 8.9 %copy-start.12 = (f32[32]{0:T(128)S(1)}, f32[32]{0:T(128)}, u32[]{:S(2)}) copy-start(f32[32]{0:T(128)} %copy-done.11) | copy-start | bytes 388
  182.0 8.9 %copy-start.14 = (bf16[2048,32]{0,1:T(8,128)(2,1)S(1)}, bf16[2048,32]{0,1:T(8,128)(2,1)}, u32[]{:S(2)}) copy-start(bf16[2048,32]{0,1:T(8,128)(2,1)} %param.16) | copy-start | bytes 393220
  182.0 9.4 %copy-start.1 = (bf16[4096,176]{0,1:T(8,128)(2,1)S(1)}, bf16[4096,176]{0,1:T(8,128)(2,1)}, u32[]{:S(2)}) copy-start(bf16[4096,176]{0,1:T(8,128)(2,1)} %all-gather.10.cloned.1.call-done) | copy-start | bytes 4325380
  183.6 9.9 %collective-permute-start.2 = (bf16[8,512,176]{1,2,0:T(8,128)(2,1)S(1)}, bf16[8,512,176]{1,2,0:T(8,128)(2,1)S(1)}, u32[]{:S(2)}, u32[]{:S(2)}) collective-permute-start(bf16[8,512,176]{1,2,0:T(8,128)(2,1)S(1)} %bitcast.83), channel_id=1, source_target_pairs={{0,32},{32,0},{64,96},{96,64},{128,160},{160,128},{192,224},{224,1... | collective-permute-start | bytes 4325384 | tf_op jit(solution)/shard_map/ppermute | solution.py:15
  193.9 1.1 copy-start.4
  223.1 16.0 %all-to-all-start.4 = ((bf16[16,32,128]{2,1,0:T(8,128)(2,1)}), bf16[16,32,128]{2,1,0:T(8,128)(2,1)}, u32[]{:S(2)}, u32[]{:S(2)}) async-start(bf16[16,32,128]{2,1,0:T(8,128)(2,1)} %bitcast.90), calls=%async_computation.4 | async-start | bytes 262144 | tf_op jit(solution)/shard_map/all_to_all | solution.py:141
  230.5 10.9 %copy-start.9 = (f32[2048]{0:T(1024)S(1)}, f32[2048]{0:T(1024)}, u32[]{:S(2)}) copy-start(f32[2048]{0:T(1024)} %param.23) | copy-start | bytes 24580
  (1 other events, 1.0 us)
Sparse Core Ops, SparseCore 0:
  9.7 83.6 all-gather.5
  96.2 36.5 all-gather.7
  145.5 36.4 all-gather.9
where the time goes:
time: 250 us; the launch traced here: 249 us
  waiting for transfers between devices  101 us (40%)
  starting transfers between devices  46.9 us (19%)
  blocking collectives  44.2 us (18%)
  matrix products  16.3 us (7%)
  between operations  15.4 us (6%)
  local copies, waits for them, and re-layouts  14.8 us (6%)
  other arithmetic  9.99 us (4%)
    all_to_all x1, blocking collectives, pair_collect(): lax.all_to_all(copies, axis, 0, 0, tiled=True, axis_index_groups=core_gro...  44.2 us
    all_gather x2, waiting for transfers between devices, pair_gather(): lax.all_gather(array, axis, axis=0, axis_index_groups=core_groups(axis))  34.7 us
    all_to_all x1, waiting for transfers between devices, per_device(): lax.all_to_all(result, 'expert', split_axis=0, concat_axis=0, tiled=True)  26.5 us
    ppermute x3, starting transfers between devices, with_sibling(): lax.ppermute(blocks, axis, [(i, i ^ 1) for i in range(lax.axis_size(axis))])  19.2 us
    all_to_all x1, starting transfers between devices, per_device(): lax.all_to_all(outgoing, 'expert', split_axis=0, concat_axis=0, tiled=True)  9.68 us
    all_to_all x1, waiting for transfers between devices, per_device(): lax.all_to_all(outgoing, 'expert', split_axis=0, concat_axis=0, tiled=True)  9.27 us
    all_to_all x1, waiting for transfers between devices, per_device(): lax.all_to_all(proj_cols, 'dp', split_axis=0, concat_axis=1, tiled=True)  8.85 us
    all_gather x1, waiting for transfers between devices, per_device(): weights_full = lax.all_gather(weights_part, 'dp', axis=0, tiled=True)  8.74 us
  transfers between devices with their start and end apart: 10, of which 10 were waited for; matrix products, arithmetic and copies ran while one was open for 13% of the time, Pallas kernels for 0%

commit v1 on v0

--- a/solution.py
+++ b/solution.py
@@ -1,9 +1,29 @@
+import functools
 import jax
 import jax.numpy as jnp
 from jax import lax
 from jax.sharding import PartitionSpec as P
 
 EPS = 1e-06
+
+
+def feed_panels(slab_in, lane_axis):
+    cores_n = jax.lax.axis_size(lane_axis)
+    rack = [(tick, (tick + 1) % cores_n) for tick in range(cores_n)]
+    local_out, u_next = ([slab_in], [slab_in])
+    all_blocks = [(tick, (tick - 1) % cores_n) for tick in range(cores_n)]
+    for _ in range(cores_n // 2):
+        back = jax.lax.ppermute(local_out[-1], axis_name=lane_axis, perm=rack)
+        local_out.append(back)
+    for _ in tuple(range((cores_n - 1) // 2)):
+        big = jax.lax.ppermute(u_next[-1], perm=all_blocks, axis_name=lane_axis)
+        u_next.append(big)
+    o_now = jnp.concatenate([*local_out[::-1], *u_next[1:]], 0)
+    f_next = jax.lax.axis_index(lane_axis)
+    return jnp.roll(o_now, shift=(f_next - cores_n // 2) * slab_in.shape[0], axis=0)
+
+
+perform_indices_on = functools.partial(feed_panels, lane_axis="dp")
 
 
 def core_groups(axis):
@@ -109,7 +129,7 @@
     outgoing = outgoing.astype(jnp.bfloat16).reshape(experts, capacity, width)
     hidden_units = expert_down.shape[1]
     weights_part = jnp.concatenate([expert_gate_up[0], expert_down[0].T], axis=1)
-    weights_full = lax.all_gather(weights_part, "dp", axis=0, tiled=True)
+    weights_full = perform_indices_on(weights_part)
     gate_up_full = weights_full[:, : 2 * hidden_units]
     down_turned_full = weights_full[:, 2 * hidden_units :]
     received = lax.all_to_all(outgoing, "expert", split_axis=0, concat_axis=0, tiled=True)

time: 250 us -> 371 us (1.48)
  waiting for transfers between devices: 101 us -> 166 us
  local copies, waits for them, and re-layouts: 14.8 us -> 71.8 us
  blocking collectives: 44.2 us -> 0 us
  starting transfers between devices: 46.9 us -> 82.8 us
  other arithmetic: 9.99 us -> 14 us
    all_to_all x1 -> x0, blocking collectives: 44.2 us -> none  [pair_collect(): lax.all_to_all(copies, axis, 0, 0, tiled=True, axis_index_groups=core_gro...]
    all_to_all x1, waiting for transfers between devices: 9.27 us -> 44.8 us  [per_device(): lax.all_to_all(outgoing, 'expert', split_axis=0, concat_axis=0, tiled=True)]
    ppermute x0 -> x15, waiting for transfers between devices: none -> 33.9 us  [the longest x8 32.1 us: feed_panels(): back = jax.lax.ppermute(local_out[-1], axis_name=lane_axis, perm=rack)]
    ppermute x0 -> x15, local copies, waits for them, and re-layouts: none -> 30.6 us  [the longest x8 15.9 us: feed_panels(): back = jax.lax.ppermute(local_out[-1], axis_name=lane_axis, perm=rack)]
    ppermute x0 -> x15, starting transfers between devices: none -> 25.9 us  [the longest x7 13.7 us: feed_panels(): big = jax.lax.ppermute(u_next[-1], perm=all_blocks, axis_name=lane_axis)]
    unnamed x32 -> x91, local copies, waits for them, and re-layouts: 2.76 us -> 27.1 us
    all_to_all x1, waiting for transfers between devices: 26.5 us -> 38.1 us  [per_device(): lax.all_to_all(result, 'expert', split_axis=0, concat_axis=0, tiled=True)]
    all_to_all x0 -> x1, starting transfers between devices: none -> 10.9 us  [pair_collect(): lax.all_to_all(copies, axis, 0, 0, tiled=True, axis_index_groups=core_gro...]
  transfers between devices with their start and end apart: 10 -> 25, of which waited for: 10 -> 11; matrix products, arithmetic and copies ran while one was open for 13% -> 19% of each run, Pallas kernels for 0% -> 0%
where the time goes in v1:
time: 371 us; the launch traced here: 369 us
  waiting for transfers between devices  166 us (45%)
  starting transfers between devices  82.8 us (22%)
  local copies, waits for them, and re-layouts  71.8 us (19%)
  matrix products  18.3 us (5%)
  between operations  16.2 us (4%)
  other arithmetic  14 us (4%)
    all_to_all x1, waiting for transfers between devices, per_device(): lax.all_to_all(outgoing, 'expert', split_axis=0, concat_axis=0, tiled=True)  44.8 us
    all_to_all x1, waiting for transfers between devices, per_device(): lax.all_to_all(result, 'expert', split_axis=0, concat_axis=0, tiled=True)  38.1 us
    all_gather x2, waiting for transfers between devices, pair_gather(): lax.all_gather(array, axis, axis=0, axis_index_groups=core_groups(axis))  35.6 us
    ppermute x8, waiting for transfers between devices, feed_panels(): back = jax.lax.ppermute(local_out[-1], axis_name=lane_axis, perm=rack)  32.1 us
    unnamed x91, local copies, waits for them, and re-layouts  27.1 us
    ppermute x8, local copies, waits for them, and re-layouts, feed_panels(): back = jax.lax.ppermute(local_out[-1], axis_name=lane_axis, perm=rack)  15.9 us
    ppermute x7, local copies, waits for them, and re-layouts, feed_panels(): big = jax.lax.ppermute(u_next[-1], perm=all_blocks, axis_name=lane_axis)  14.7 us
    ppermute x3, starting transfers between devices, with_sibling(): lax.ppermute(blocks, axis, [(i, i ^ 1) for i in range(lax.axis_size(axis))])  14.6 us
  transfers between devices with their start and end apart: 25, of which 11 were waited for; matrix products, arithmetic and copies ran while one was open for 19% of the time, Pallas kernels for 0%

profile of v1, /device:TPU:1, one launch (start us, length us, event | category | flops | bytes accessed | tf_op | source)
XLA Modules:
  0.0 369.0 jit_solution(14875731956277678673)
XLA Ops:
  8.6 10.9 %all-to-all-start = ((bf16[8,32,2048]{2,1,0:T(8,128)(2,1)}), bf16[8,32,2048]{2,1,0:T(8,128)(2,1)S(1)}, u32[]{:S(2)}, u32[]{:S(2)}) async-start(bf16[8,32,2048]{2,1,0:T(8,128)(2,1)} %broadcast_in_dim.26), calls=%async_computation | async-start | bytes 2097152 | tf_op jit(solution)/shard_map/all_to_all | solution.py:48
  22.7 2.6 collective-permute-start.1
  25.3 23.3 %collective-permute-done.1 = bf16[128,2112]{0,1:T(8,128)(2,1)S(1)} collective-permute-done((bf16[128,2112]{0,1:T(8,128)(2,1)}, bf16[128,2112]{0,1:T(8,128)(2,1)S(1)}, u32[]{:S(2)}, u32[]{:S(2)}) %collective-permute-start.1) | collective-permute-done | bytes 540704 | tf_op jit(solution)/shard_map/ppermute | solution.py:16
  52.3 5.0 %collective-permute-done.2 = bf16[128,2112]{0,1:T(8,128)(2,1)S(1)} collective-permute-done((bf16[128,2112]{0,1:T(8,128)(2,1)S(1)}, bf16[128,2112]{0,1:T(8,128)(2,1)S(1)}, u32[]{:S(2)}, u32[]{:S(2)}) %collective-permute-start.2) | collective-permute-done | bytes 540704 | tf_op jit(solution)/shard_map/ppermute | solution.py:16
  62.3 3.8 %collective-permute-done.3 = bf16[128,2112]{0,1:T(8,128)(2,1)} collective-permute-done((bf16[128,2112]{0,1:T(8,128)(2,1)S(1)}, bf16[128,2112]{0,1:T(8,128)(2,1)}, u32[]{:S(2)}, u32[]{:S(2)}) %collective-permute-start.3) | collective-permute-done | bytes 540704 | tf_op jit(solution)/shard_map/ppermute | solution.py:16
  66.1 2.6 collective-permute-start.4
  69.3 3.1 collective-permute-start.12
  72.4 4.8 %collective-permute-start = (bf16[8,32,2048]{2,1,0:T(8,128)(2,1)S(1)}, bf16[8,32,2048]{2,1,0:T(8,128)(2,1)}, u32[]{:S(2)}, u32[]{:S(2)}) collective-permute-start(bf16[8,32,2048]{2,1,0:T(8,128)(2,1)S(1)} %all-to-all-done), channel_id=1, source_target_pairs={{0,32},{32,0},{64,96},{96,64},{128,160},{160,128},{192,224},{224,1... | collective-permute-start | bytes 3145736 | tf_op jit(solution)/shard_map/ppermute | solution.py:35
  78.7 4.0 %collective-permute-start.13 = (bf16[128,2112]{0,1:T(8,128)(2,1)}, bf16[128,2112]{0,1:T(8,128)(2,1)}, u32[]{:S(2)}, u32[]{:S(2)}) collective-permute-start(bf16[128,2112]{0,1:T(8,128)(2,1)} %collective-permute-done.12), channel_id=1, source_target_pairs={{0,480},{32,0},{64,32},{96,64},{128,96},{160,128},{192,160},{224,1... | collective-permute-start | bytes 1622024 | tf_op jit(solution)/shard_map/ppermute | solution.py:19
  102.8 3.0 collective-permute-start.14
  113.8 7.8 %all-to-all-start.1 = ((bf16[16,32,128]{2,1,0:T(8,128)(2,1)}), bf16[16,32,128]{2,1,0:T(8,128)(2,1)S(1)}, u32[]{:S(2)}, u32[]{:S(2)}) async-start(bf16[16,32,128]{2,1,0:T(8,128)(2,1)} %bitcast.4), calls=%async_computation.1 | async-start | bytes 262144 | tf_op jit(solution)/shard_map/all_to_all | solution.py:111
  123.5 6.2 %all-to-all-done.1 = bf16[16,32,128]{2,1,0:T(8,128)(2,1)S(1)} async-done(((bf16[16,32,128]{2,1,0:T(8,128)(2,1)}), bf16[16,32,128]{2,1,0:T(8,128)(2,1)S(1)}, u32[]{:S(2)}, u32[]{:S(2)}) %all-to-all-start.1) | async-done | bytes 131104 | tf_op jit(solution)/shard_map/all_to_all | solution.py:111
  164.1 6.1 %copy-done.26 = bf16[4096,2112]{1,0:T(8,128)(2,1)} copy-done((bf16[4096,2112]{1,0:T(8,128)(2,1)}, bf16[4096,2112]{1,0:T(8,128)(2,1)S(1)}, u32[]{:S(2)}) %copy-start.26) | copy-done | bytes 17301528
  173.1 35.6 %all-gather.5.cloned.1.call-done = bf16[256,2048]{1,0:T(8,128)(2,1)} async-done(((bf16[32,2048]{1,0:T(8,128)(2,1)}), bf16[256,2048]{1,0:T(8,128)(2,1)}) %all-gather.5.cloned.1.call-update) | async-done | bytes 1048592 | tf_op jit(solution)/shard_map/all_gather | solution.py:42
  208.7 7.1 %collective-permute-start.16 = (bf16[8,32,2048]{2,1,0:T(8,128)(2,1)}, bf16[8,32,2048]{2,1,0:T(8,128)(2,1)}, u32[]{:S(2)}, u32[]{:S(2)}) collective-permute-start(bf16[8,32,2048]{2,1,0:T(8,128)(2,1)} %bitcast.91), channel_id=1, source_target_pairs={{0,32},{32,0},{64,96},{96,64},{128,160},{160,128},{192,224},{224,1... | collective-permute-start | bytes 3145736 | tf_op jit(solution)/shard_map/ppermute | solution.py:35
  215.8 9.3 %all-to-all-start.2 = ((bf16[32,12,2048]{2,1,0:T(8,128)(2,1)}), bf16[32,12,2048]{2,1,0:T(8,128)(2,1)S(1)}, u32[]{:S(2)}, u32[]{:S(2)}) async-start(bf16[32,12,2048]{2,1,0:T(8,128)(2,1)} %reshape.112), calls=%async_computation.2 | async-start | bytes 4194304 | tf_op jit(solution)/shard_map/all_to_all | solution.py:135
  229.5 44.8 %all-to-all-done.2 = bf16[32,12,2048]{2,1,0:T(8,128)(2,1)S(1)} async-done(((bf16[32,12,2048]{2,1,0:T(8,128)(2,1)}), bf16[32,12,2048]{2,1,0:T(8,128)(2,1)S(1)}, u32[]{:S(2)}, u32[]{:S(2)}) %all-to-all-start.2) | async-done | bytes 1572896 | tf_op jit(solution)/shard_map/all_to_all | solution.py:135
  275.6 5.7 %fusion = f32[384,1408]{1,0:T(8,128)S(1)} fusion(bf16[384,2048]{1,0:T(8,128)(2,1)} %reshape.113, bf16[4096,2112]{1,0:T(8,128)(2,1)} %copy-done.26, s32[]{:T(128)S(6)} %select_n.57), kind=kOutput, calls=%fused_computation | convolution fusion | flops 2214592512 | bytes 9502724 | tf_op jit(solution)/shard_map/dot_general | solution.py:138
  281.3 3.4 fusion.4
  286.3 7.6 %all-to-all-start.3 = ((bf16[32,12,2048]{2,1,0:T(8,128)(2,1)}), bf16[32,12,2048]{2,1,0:T(8,128)(2,1)S(1)}, u32[]{:S(2)}, u32[]{:S(2)}) async-start(bf16[32,12,2048]{2,1,0:T(8,128)(2,1)} %reshape.114), calls=%async_computation.3 | async-start | bytes 4194304 | tf_op jit(solution)/shard_map/all_to_all | solution.py:144
  295.5 2.6 collective-permute-start.17
  304.4 38.1 %all-to-all-done.3 = bf16[32,12,2048]{2,1,0:T(8,128)(2,1)S(1)} async-done(((bf16[32,12,2048]{2,1,0:T(8,128)(2,1)}), bf16[32,12,2048]{2,1,0:T(8,128)(2,1)S(1)}, u32[]{:S(2)}, u32[]{:S(2)}) %all-to-all-start.3) | async-done | bytes 1572896 | tf_op jit(solution)/shard_map/all_to_all | solution.py:144
  342.6 6.5 %all-to-all-start.4 = ((bf16[16,32,128]{2,1,0:T(8,128)(2,1)}), bf16[16,32,128]{2,1,0:T(8,128)(2,1)}, u32[]{:S(2)}, u32[]{:S(2)}) async-start(bf16[16,32,128]{2,1,0:T(8,128)(2,1)} %bitcast.93), calls=%async_computation.4 | async-start | bytes 262144 | tf_op jit(solution)/shard_map/all_to_all | solution.py:161
  351.1 7.2 %all-to-all-done.4 = bf16[16,32,128]{2,1,0:T(8,128)(2,1)} async-done(((bf16[16,32,128]{2,1,0:T(8,128)(2,1)}), bf16[16,32,128]{2,1,0:T(8,128)(2,1)}, u32[]{:S(2)}, u32[]{:S(2)}) %all-to-all-start.4) | async-done | bytes 131104 | tf_op jit(solution)/shard_map/all_to_all | solution.py:161
  (189 shorter events, 101.6 us)
Async XLA Ops:
  8.6 63.8 %all-to-all-start = ((bf16[8,32,2048]{2,1,0:T(8,128)(2,1)}), bf16[8,32,2048]{2,1,0:T(8,128)(2,1)S(1)}, u32[]{:S(2)}, u32[]{:S(2)}) async-start(bf16[8,32,2048]{2,1,0:T(8,128)(2,1)} %broadcast_in_dim.26), calls=%async_computation | async-start | bytes 2097152 | tf_op jit(solution)/shard_map/all_to_all | solution.py:48
  22.7 25.9 %collective-permute-start.1 = (bf16[128,2112]{0,1:T(8,128)(2,1)}, bf16[128,2112]{0,1:T(8,128)(2,1)S(1)}, u32[]{:S(2)}, u32[]{:S(2)}) collective-permute-start(bf16[128,2112]{0,1:T(8,128)(2,1)} %copy.76), channel_id=1, source_target_pairs={{0,32},{32,64},{64,96},{96,128},{128,160},{160,192},{192,224},{224... | collective-permute-start | bytes 1622024 | tf_op jit(solution)/shard_map/ppermute | solution.py:16
  25.3 25.7 %collective-permute-start.9 = (bf16[128,2112]{0,1:T(8,128)(2,1)}, bf16[128,2112]{0,1:T(8,128)(2,1)S(1)}, u32[]{:S(2)}, u32[]{:S(2)}) collective-permute-start(bf16[128,2112]{0,1:T(8,128)(2,1)} %copy.76), channel_id=1, source_target_pairs={{0,480},{32,0},{64,32},{96,64},{128,96},{160,128},{192,160},{224,1... | collective-permute-start | bytes 1622024 | tf_op jit(solution)/shard_map/ppermute | solution.py:19
  48.6 8.7 %collective-permute-start.2 = (bf16[128,2112]{0,1:T(8,128)(2,1)S(1)}, bf16[128,2112]{0,1:T(8,128)(2,1)S(1)}, u32[]{:S(2)}, u32[]{:S(2)}) collective-permute-start(bf16[128,2112]{0,1:T(8,128)(2,1)S(1)} %collective-permute-done.1), channel_id=1, source_target_pairs={{0,32},{32,64},{64,96},{96,128},{128,160},{160,192},{192,224},{224... | collective-permute-start | bytes 1622024 | tf_op jit(solution)/shard_map/ppermute | solution.py:16
  51.0 9.1 %collective-permute-start.10 = (bf16[128,2112]{0,1:T(8,128)(2,1)S(1)}, bf16[128,2112]{0,1:T(8,128)(2,1)S(1)}, u32[]{:S(2)}, u32[]{:S(2)}) collective-permute-start(bf16[128,2112]{0,1:T(8,128)(2,1)S(1)} %collective-permute-done.9), channel_id=1, source_target_pairs={{0,480},{32,0},{64,32},{96,64},{128,96},{160,128},{192,160},{224,1... | collective-permute-start | bytes 1622024 | tf_op jit(solution)/shard_map/ppermute | solution.py:19
  57.3 8.8 %collective-permute-start.3 = (bf16[128,2112]{0,1:T(8,128)(2,1)S(1)}, bf16[128,2112]{0,1:T(8,128)(2,1)}, u32[]{:S(2)}, u32[]{:S(2)}) collective-permute-start(bf16[128,2112]{0,1:T(8,128)(2,1)S(1)} %collective-permute-done.2), channel_id=1, source_target_pairs={{0,32},{32,64},{64,96},{96,128},{128,160},{160,192},{192,224},{224... | collective-permute-start | bytes 1622024 | tf_op jit(solution)/shard_map/ppermute | solution.py:16
  60.1 9.2 %collective-permute-start.11 = (bf16[128,2112]{0,1:T(8,128)(2,1)S(1)}, bf16[128,2112]{0,1:T(8,128)(2,1)}, u32[]{:S(2)}, u32[]{:S(2)}) collective-permute-start(bf16[128,2112]{0,1:T(8,128)(2,1)S(1)} %collective-permute-done.10), channel_id=1, source_target_pairs={{0,480},{32,0},{64,32},{96,64},{128,96},{160,128},{192,160},{224,1... | collective-permute-start | bytes 1622024 | tf_op jit(solution)/shard_map/ppermute | solution.py:19
  66.1 11.2 %collective-permute-start.4 = (bf16[128,2112]{0,1:T(8,128)(2,1)}, bf16[128,2112]{0,1:T(8,128)(2,1)}, u32[]{:S(2)}, u32[]{:S(2)}) collective-permute-start(bf16[128,2112]{0,1:T(8,128)(2,1)} %collective-permute-done.3), channel_id=1, source_target_pairs={{0,32},{32,64},{64,96},{96,128},{128,160},{160,192},{192,224},{224... | collective-permute-start | bytes 1622024 | tf_op jit(solution)/shard_map/ppermute | solution.py:16
  69.3 9.4 %collective-permute-start.12 = (bf16[128,2112]{0,1:T(8,128)(2,1)}, bf16[128,2112]{0,1:T(8,128)(2,1)}, u32[]{:S(2)}, u32[]{:S(2)}) collective-permute-start(bf16[128,2112]{0,1:T(8,128)(2,1)} %collective-permute-done.11), channel_id=1, source_target_pairs={{0,480},{32,0},{64,32},{96,64},{128,96},{160,128},{192,160},{224,1... | collective-permute-start | bytes 1622024 | tf_op jit(solution)/shard_map/ppermute | solution.py:19
  72.4 33.3 %collective-permute-start = (bf16[8,32,2048]{2,1,0:T(8,128)(2,1)S(1)}, bf16[8,32,2048]{2,1,0:T(8,128)(2,1)}, u32[]{:S(2)}, u32[]{:S(2)}) collective-permute-start(bf16[8,32,2048]{2,1,0:T(8,128)(2,1)S(1)} %all-to-all-done), channel_id=1, source_target_pairs={{0,32},{32,0},{64,96},{96,64},{128,160},{160,128},{192,224},{224,1... | collective-permute-start | bytes 3145736 | tf_op jit(solution)/shard_map/ppermute | solution.py:35
  77.3 21.2 %collective-permute-start.5 = (bf16[128,2112]{0,1:T(8,128)(2,1)}, bf16[128,2112]{0,1:T(8,128)(2,1)}, u32[]{:S(2)}, u32[]{:S(2)}) collective-permute-start(bf16[128,2112]{0,1:T(8,128)(2,1)} %collective-permute-done.4), channel_id=1, source_target_pairs={{0,32},{32,64},{64,96},{96,128},{128,160},{160,192},{192,224},{224... | collective-permute-start | bytes 1622024 | tf_op jit(solution)/shard_map/ppermute | solution.py:16
  78.7 22.0 %collective-permute-start.13 = (bf16[128,2112]{0,1:T(8,128)(2,1)}, bf16[128,2112]{0,1:T(8,128)(2,1)}, u32[]{:S(2)}, u32[]{:S(2)}) collective-permute-start(bf16[128,2112]{0,1:T(8,128)(2,1)} %collective-permute-done.12), channel_id=1, source_target_pairs={{0,480},{32,0},{64,32},{96,64},{128,96},{160,128},{192,160},{224,1... | collective-permute-start | bytes 1622024 | tf_op jit(solution)/shard_map/ppermute | solution.py:19
  98.5 14.9 %collective-permute-start.6 = (bf16[128,2112]{0,1:T(8,128)(2,1)}, bf16[128,2112]{0,1:T(8,128)(2,1)}, u32[]{:S(2)}, u32[]{:S(2)}) collective-permute-start(bf16[128,2112]{0,1:T(8,128)(2,1)} %collective-permute-done.5), channel_id=1, source_target_pairs={{0,32},{32,64},{64,96},{96,128},{128,160},{160,192},{192,224},{224... | collective-permute-start | bytes 1622024 | tf_op jit(solution)/shard_map/ppermute | solution.py:16
  102.8 19.0 %collective-permute-start.14 = (bf16[128,2112]{0,1:T(8,128)(2,1)}, bf16[128,2112]{0,1:T(8,128)(2,1)}, u32[]{:S(2)}, u32[]{:S(2)}) collective-permute-start(bf16[128,2112]{0,1:T(8,128)(2,1)} %collective-permute-done.13), channel_id=1, source_target_pairs={{0,480},{32,0},{64,32},{96,64},{128,96},{160,128},{192,160},{224,1... | collective-permute-start | bytes 1622024 | tf_op jit(solution)/shard_map/ppermute | solution.py:19
  113.5 8.4 %collective-permute-start.7 = (bf16[128,2112]{0,1:T(8,128)(2,1)}, bf16[128,2112]{0,1:T(8,128)(2,1)}, u32[]{:S(2)}, u32[]{:S(2)}) collective-permute-start(bf16[128,2112]{0,1:T(8,128)(2,1)} %collective-permute-done.6), channel_id=1, source_target_pairs={{0,32},{32,64},{64,96},{96,128},{128,160},{160,192},{192,224},{224... | collective-permute-start | bytes 1622024 | tf_op jit(solution)/shard_map/ppermute | solution.py:16
  113.8 16.0 %all-to-all-start.1 = ((bf16[16,32,128]{2,1,0:T(8,128)(2,1)}), bf16[16,32,128]{2,1,0:T(8,128)(2,1)S(1)}, u32[]{:S(2)}, u32[]{:S(2)}) async-start(bf16[16,32,128]{2,1,0:T(8,128)(2,1)} %bitcast.4), calls=%async_computation.1 | async-start | bytes 262144 | tf_op jit(solution)/shard_map/all_to_all | solution.py:111
  121.6 87.1 %all-gather.5.cloned.1.call-start = ((), (), s32[]{:S(2)}) async-start(), calls=%async_computation.5 | async-start | bytes 1179648 | tf_op jit(solution)/shard_map/all_gather | solution.py:42
  121.8 19.3 %collective-permute-start.15 = (bf16[128,2112]{0,1:T(8,128)(2,1)}, bf16[128,2112]{0,1:T(8,128)(2,1)}, u32[]{:S(2)}, u32[]{:S(2)}) collective-permute-start(bf16[128,2112]{0,1:T(8,128)(2,1)} %collective-permute-done.14), channel_id=1, source_target_pairs={{0,480},{32,0},{64,32},{96,64},{128,96},{160,128},{192,160},{224,1... | collective-permute-start | bytes 1622024 | tf_op jit(solution)/shard_map/ppermute | solution.py:19
  121.9 21.3 %collective-permute-start.8 = (bf16[128,2112]{0,1:T(8,128)(2,1)}, bf16[128,2112]{0,1:T(8,128)(2,1)}, u32[]{:S(2)}, u32[]{:S(2)}) collective-permute-start(bf16[128,2112]{0,1:T(8,128)(2,1)} %collective-permute-done.7), channel_id=1, source_target_pairs={{0,32},{32,64},{64,96},{96,128},{128,160},{160,192},{192,224},{224... | collective-permute-start | bytes 1622024 | tf_op jit(solution)/shard_map/ppermute | solution.py:16
  208.7 16.7 %collective-permute-start.16 = (bf16[8,32,2048]{2,1,0:T(8,128)(2,1)}, bf16[8,32,2048]{2,1,0:T(8,128)(2,1)}, u32[]{:S(2)}, u32[]{:S(2)}) collective-permute-start(bf16[8,32,2048]{2,1,0:T(8,128)(2,1)} %bitcast.91), channel_id=1, source_target_pairs={{0,32},{32,0},{64,96},{96,64},{128,160},{160,128},{192,224},{224,1... | collective-permute-start | bytes 3145736 | tf_op jit(solution)/shard_map/ppermute | solution.py:35
  215.8 58.4 %all-to-all-start.2 = ((bf16[32,12,2048]{2,1,0:T(8,128)(2,1)}), bf16[32,12,2048]{2,1,0:T(8,128)(2,1)S(1)}, u32[]{:S(2)}, u32[]{:S(2)}) async-start(bf16[32,12,2048]{2,1,0:T(8,128)(2,1)} %reshape.112), calls=%async_computation.2 | async-start | bytes 4194304 | tf_op jit(solution)/shard_map/all_to_all | solution.py:135
  225.1 68.8 %all-gather.7.cloned.1.call-start = ((), (), s32[]{:S(2)}) async-start(), calls=%async_computation.6 | async-start | bytes 1622016 | tf_op jit(solution)/shard_map/all_gather | solution.py:42
  286.3 56.3 %all-to-all-start.3 = ((bf16[32,12,2048]{2,1,0:T(8,128)(2,1)}), bf16[32,12,2048]{2,1,0:T(8,128)(2,1)S(1)}, u32[]{:S(2)}, u32[]{:S(2)}) async-start(bf16[32,12,2048]{2,1,0:T(8,128)(2,1)} %reshape.114), calls=%async_computation.3 | async-start | bytes 4194304 | tf_op jit(solution)/shard_map/all_to_all | solution.py:144
  342.6 15.7 %all-to-all-start.4 = ((bf16[16,32,128]{2,1,0:T(8,128)(2,1)}), bf16[16,32,128]{2,1,0:T(8,128)(2,1)}, u32[]{:S(2)}, u32[]{:S(2)}) async-start(bf16[16,32,128]{2,1,0:T(8,128)(2,1)} %bitcast.93), calls=%async_computation.4 | async-start | bytes 262144 | tf_op jit(solution)/shard_map/all_to_all | solution.py:161
  (31 other events, 1195.3 us)
Sparse Core Ops, SparseCore 0:
  173.2 35.4 all-gather.4
  229.6 37.2 all-gather.6
